TPU v7x, 32 devices: a whole 2x2x4 slice. The times are simulated.
32 devices in a mesh: groups: 2 (over y), events: 8 (over z, x), heads: 2 (over core).
Axes of the slice: x: 2, y: 2, z: 4, core: 2. Of those that a mesh axis runs over, the one named last changes fastest.
Arguments:
- inputs: bfloat16 [256, 1024], P(('groups', 'events')), parts along dimension 0, may hold values from -6 to 6
- cand_user: int32 [256], P('groups'), parts along dimension 0, may hold values from 0 to 3, as said below
- event_user: int32 [8192], P(('groups', 'events')), parts along dimension 0, may hold values from 0 to 3, as said below
- event_count: int32 [16], P(('groups', 'events')), parts along dimension 0, may hold values from 128 to 512, as said below
- w_qu: bfloat16 [1024, 2, 1024], P(None, None, 'heads'), may hold values from -0.1875 to 0.1875
- keys: bfloat16 [8192, 1024], P(('groups', 'events'), 'heads'), parts along dimension 0, may hold values from -6 to 6
- values: bfloat16 [8192, 1024], P(('groups', 'events'), 'heads'), parts along dimension 0, may hold values from -6 to 6
- gain: float32 [1024], P('heads'), may hold values from 0.1 to 1.9
- w_out: bfloat16 [1024, 1024], P('heads'), may hold values from -0.1875 to 0.1875
Outputs:
- scored: bfloat16 [256, 1024], P(('groups', 'events')), parts along dimension 0
There are 2 independent parts, one for each index of `groups`. A program takes and returns all parts, laid end to end along the dimension named above; an argument that names none is the same for every part. Nothing has to cross between parts.
Inputs may be any that keep to these rules, and one draw needn't show every extreme that they name: `event_count`: each cache shard's filled slots come first; some shard is full and some holds 128. `event_user`: Users' events are consecutive and in increasing user order over the whole cache; every user has 1 to 2047 events, and some user has exactly 2047. `cand_user`: every candidate belongs to a user that has at least one filled slot somewhere in the cache.
All inputs are finite; a program needn't handle non-finite values.
Results may differ from a plain program's by a relative error of at most 0.0075.
Values may be sent and summed in bfloat16 or wider, within the bound.
No kernel may reach another device: no remote copies, remote signals or barrier semaphores. Data moves between devices by JAX's collectives and lax.ppermute only.
A program may use at most 64 MiB of HBM per device.

v0:
```python
import math
import jax
import jax.numpy as jnp
from jax import lax
from jax.sharding import PartitionSpec as P

DH = 128
HD = 1024
epsilon = 1e-05


def shards(inputs, cand_user, event_user, event_count, w_qu, keys, values, gain, w_out):
    row_count = inputs.shape[0]
    feat_width = inputs.shape[1]
    local_width = w_qu.shape[2]
    heads_here = local_width // DH
    slot_total = keys.shape[0]
    score_scale = 1.0 / math.sqrt(DH)
    packed_weight = w_qu.reshape(feat_width, 2 * local_width)
    query_weight = packed_weight[:, :local_width]
    gate_weight = packed_weight[:, local_width:]
    gate_values = jax.nn.silu(
        jnp.dot(inputs, gate_weight, preferred_element_type=jnp.float32)
    ).astype(jnp.bfloat16)
    gathered_rows = lax.all_gather(inputs, "events", axis=0, tiled=True)
    queries = jax.nn.silu(
        jnp.dot(gathered_rows, query_weight, preferred_element_type=jnp.float32)
    ).astype(jnp.bfloat16)
    slot_index = jnp.arange(slot_total, dtype=jnp.int32)
    slot_valid = slot_index < event_count[0]
    key_heads = keys.reshape(slot_total, heads_here, DH)
    value_heads = values.reshape(slot_total, heads_here, DH)

    def attend_rows(query_rows, row_users):
        rows_here = query_rows.shape[0]
        query_block = query_rows.reshape(rows_here, heads_here, DH)
        user_match = ((row_users[:, None] == event_user[None, :]) & slot_valid[None, :]).astype(
            jnp.float32
        )
        scores = (
            jnp.einsum("chd,ehd->hce", query_block, key_heads, preferred_element_type=jnp.float32)
            * score_scale
        )
        attn_weights = (jax.nn.silu(scores) * user_match[None]).astype(jnp.bfloat16)
        partial_out = jnp.einsum(
            "hce,ehd->chd", attn_weights, value_heads, preferred_element_type=jnp.float32
        )
        return partial_out.reshape(rows_here, local_width)

    block_rows = math.gcd(row_count * lax.axis_size("events"), 512)
    block_count = row_count * lax.axis_size("events") // block_rows

    def compute_block(which_block):
        block_start = which_block * block_rows
        query_rows = lax.dynamic_slice_in_dim(queries, block_start, block_rows, 0)
        block_users = lax.dynamic_slice_in_dim(cand_user, block_start, block_rows, 0)
        return attend_rows(query_rows, block_users)

    stacked = lax.map(compute_block, jnp.arange(block_count, dtype=jnp.int32))
    attended = lax.psum_scatter(
        stacked.reshape(row_count * lax.axis_size("events"), local_width),
        "events",
        scatter_dimension=0,
        tiled=True,
    )
    first_moment = jnp.sum(attended, axis=1)
    second_moment = jnp.sum(attended * attended, axis=1)
    total_first, total_second = lax.psum((first_moment, second_moment), "heads")
    average = total_first / HD
    variance = total_second / HD - average * average
    normed = (attended - average[:, None]) * lax.rsqrt(variance + epsilon)[:, None] * gain
    gated = (normed * gate_values.astype(jnp.float32)).astype(jnp.bfloat16)
    projected = jnp.dot(gated, w_out, preferred_element_type=jnp.float32)
    summed_heads = lax.psum(projected, "heads")
    return (inputs.astype(jnp.float32) + summed_heads).astype(jnp.bfloat16)


def solution(mesh):
    placed = (
        P(("groups", "events"), None),
        P("groups"),
        P(("groups", "events")),
        P(("groups", "events")),
        P(None, None, "heads"),
        P(("groups", "events"), "heads"),
        P(("groups", "events"), "heads"),
        P("heads"),
        P("heads", None),
    )
    return jax.shard_map(
        shards, mesh=mesh, in_specs=placed, out_specs=P(("groups", "events"), None), check_vma=False
    )
```

profile of v0, /device:TPU:0, one launch (start us, length us, event | category | flops | bytes accessed | tf_op | source)
XLA Modules:
  0.0 143.9 jit_solution(11439747766623471906)
XLA Ops:
  6.5 0.0 copy-start
  6.5 0.0 reduce-scatter.2.cloned.1.call-start
  7.3 32.8 %all_gather.3 = bf16[128,1024]{1,0:T(8,128)(2,1)S(1)} all-gather(bf16[16,1024]{1,0:T(8,128)(2,1)} %param.9), channel_id=1, replica_groups=mesh['groups'=2,'events'=8,'heads'=2] {'events'}, dimensions={0}, use_global_device_ids=true | all-gather | bytes 294912 | tf_op jit(solution)/shard_map/all_gather | solution.py:25
  40.1 2.0 %copy.14 = bf16[512,512]{0,1:T(8,128)(2,1)} copy(bf16[512,512]{1,0:T(8,128)(2,1)} %param.15) | data formatting | bytes 1048576 | tf_op jit(solution)/shard_map/reshape | solution.py:32
  42.1 2.2 %copy.17 = bf16[128,8,2,512]{3,1,2,0:T(8,128)(2,1)S(1)} copy(bf16[128,8,2,512]{3,2,1,0:T(2,128)(2,1)} %bitcast.29) | data formatting | bytes 4194304
  44.3 0.0 copy-start.2
  44.3 0.0 copy-start.4
  44.3 1.0 fusion.14
  45.3 0.0 copy-done.2
  45.3 0.0 copy-done.4
  45.3 0.1 and_convert_fusion
  45.4 0.0 copy-start.1
  45.4 0.0 copy-start.3
  45.4 2.6 %fusion.4 = f32[4,128,128]{1,2,0:T(8,128)} fusion(bf16[512,4,128]{0,2,1:T(8,128)(2,1)} %bitcast.30, f32[128,512]{1,0:T(8,128)S(1)} %and_convert_fusion, bf16[16,4,8,128]{3,2,1,0:T(8,128)(2,1)} %fusion.14, bf16[512,512]{1,0:T(8,128)(2,1)} %param.14), kind=kOutput, calls=%fused_computation.6 | convolution fusion | flops 136052736 | bytes 1703936 | tf_op jit(solution)/shard_map/while/body/eval_jaxpr/hce,ehd->chd/dot_general | solution.py:45
  48.1 1.8 %copy.13 = f32[128,512]{1,0:T(8,128)} copy(f32[128,512]{0,1:T(8,128)} %bitcast.31) | data formatting | bytes 524288 | tf_op jit(solution)/shard_map/reshape | solution.py:61
  49.9 0.0 reduce-scatter.2.cloned.1.call-update
  49.9 0.0 all-reduce.3.cloned.1.call-start
  49.9 63.5 %reduce-scatter.2.cloned.1.call-done = f32[16,512]{1,0:T(8,128)} async-done(((f32[128,512]{1,0:T(8,128)}), f32[16,512]{1,0:T(8,128)}) %reduce-scatter.2.cloned.1.call-update) | async-done | bytes 32784 | tf_op jit(solution)/shard_map/reduce_scatter | solution.py:60
  113.5 0.9 fusion.38
  114.3 2.5 %all-reduce = (f32[16]{0:T(128)S(1)}, f32[16]{0:T(128)S(1)}) all-reduce(f32[16]{0:T(128)S(1)} %get-tuple-element.20, f32[16]{0:T(128)S(1)} %get-tuple-element.19), channel_id=1, replica_groups=mesh['groups'=2,'events'=8,'heads'=2] {'heads'}, use_global_device_ids=true, to_apply=%region_4.5 | all-reduce | flops 32 | bytes 256 | tf_op jit(solution)/shard_map/psum | solution.py:68
  116.8 0.0 copy-done
  116.8 0.0 copy-done.1
  116.8 0.0 copy-done.3
  116.8 1.9 %fusion.26 = f32[16,1024]{1,0:T(8,128)} fusion(bf16[512,1024]{1,0:T(8,128)(2,1)S(1)} %copy-done, bf16[16,1024]{1,0:T(8,128)(2,1)S(1)} %copy-done.1, bf16[1024,1024]{1,0:T(8,128)(2,1)S(1)} %bitcast.28, f32[16,512]{1,0:T(8,128)} %reduce-scatter.2.cloned.1.call-done, f32[512]{0:T(512)S(1)} %copy-done.3, f32[16]{0:T(128)S(1)} %get-tuple-element.32, ...), kind=kOutput, calls=%fused_computation.20 | convolution fusion | flops 33644544 | bytes 2231296 | tf_op jit(solution)/shard_map/dot_general | solution.py:73
  118.7 0.0 all-reduce.3.cloned.1.call-update
  118.7 16.9 %all-reduce.3.cloned.1.call-done = f32[16,1024]{1,0:T(8,128)} async-done(((f32[16,1024]{1,0:T(8,128)}), f32[16,1024]{1,0:T(8,128)}) %all-reduce.3.cloned.1.call-update) | async-done | bytes 65552 | tf_op jit(solution)/shard_map/psum | solution.py:74
  135.6 1.5 %add_convert_fusion = bf16[16,1024]{1,0:T(8,128)(2,1)} fusion(f32[16,1024]{1,0:T(8,128)} %all-reduce.3.cloned.1.call-done, bf16[16,1024]{1,0:T(8,128)(2,1)S(1)} %copy-done.1), kind=kLoop, calls=%fused_computation.17 | loop fusion | flops 49152 | bytes 131072 | tf_op jit(solution)/shard_map/convert_element_type | solution.py:75
  (2 shorter events, 0.0 us)
Async XLA Ops:
  6.5 110.3 %copy-start = (bf16[512,1024]{1,0:T(8,128)(2,1)S(1)}, bf16[512,1024]{1,0:T(8,128)(2,1)}, u32[]{:S(2)}) copy-start(bf16[512,1024]{1,0:T(8,128)(2,1)} %param.17) | copy-start | bytes 3145732
  6.5 106.9 %reduce-scatter.2.cloned.1.call-start = ((), (), s32[]{:S(2)}) async-start(), calls=%async_computation.1 | async-start | bytes 294912 | tf_op jit(solution)/shard_map/reduce_scatter | solution.py:60
  44.3 1.0 copy-start.2
  44.3 1.0 copy-start.4
  45.4 71.4 %copy-start.1 = (bf16[16,1024]{1,0:T(8,128)(2,1)S(1)}, bf16[16,1024]{1,0:T(8,128)(2,1)}, u32[]{:S(2)}) copy-start(bf16[16,1024]{1,0:T(8,128)(2,1)} %param.9) | copy-start | bytes 98308
  45.4 71.4 %copy-start.3 = (f32[512]{0:T(512)S(1)}, f32[512]{0:T(512)}, u32[]{:S(2)}) copy-start(f32[512]{0:T(512)} %param.16) | copy-start | bytes 6148
  49.9 85.7 %all-reduce.3.cloned.1.call-start = ((), (), s32[]{:S(2)}) async-start(), calls=%async_computation.2 | async-start | bytes 131072 | tf_op jit(solution)/shard_map/psum | solution.py:74
Sparse Core Ops, SparseCore 0:
  50.0 63.4 reduce-scatter.1
  118.8 16.7 all-reduce.2
where the time goes:
time: 144 us
  waiting for transfers between devices  80.5 us (56%)
  blocking collectives  35.2 us (24%)
  between operations  14.2 us (10%)
  local copies, waits for them, and re-layouts  6 us (4%)
  matrix products  5.52 us (4%)
  other arithmetic  2.45 us (2%)
    reduce_scatter x1, waiting for transfers between devices, shards(): lax.psum_scatter(stacked.reshape(row_count * lax.axis_size('events'), loc...  63.5 us
    all_gather x1, blocking collectives, shards(): gathered_rows = lax.all_gather(inputs, 'events', axis=0, tiled=True)  32.8 us
    psum x1, waiting for transfers between devices, shards(): summed_heads = lax.psum(projected, 'heads')  16.9 us
  transfers between devices with their start and end apart: 2, of which 2 were waited for; matrix products, arithmetic and copies ran while one was open for 0% of the time, Pallas kernels for 0%

commit v1 on v0

--- a/solution.py
+++ b/solution.py
@@ -7,6 +7,27 @@
 DH = 128
 HD = 1024
 epsilon = 1e-05
+
+
+def in_order(tiles, dim):
+    tiles = jnp.moveaxis(tiles, 0, dim)
+    shape = tiles.shape
+    return tiles.reshape(*shape[:dim], shape[dim] * shape[dim + 1], *shape[dim + 2 :])
+
+
+def grow_blocks(shard, axis):
+    size, place = (lax.axis_size(axis), lax.axis_index(axis))
+    tiles, apart = (shard[None], 1)
+    while apart < size:
+        theirs = lax.ppermute(tiles, axis, [(i, i ^ apart) for i in range(size)])
+        low = place & apart == 0
+        tiles = jnp.concatenate([jnp.where(low, tiles, theirs), jnp.where(low, theirs, tiles)])
+        apart *= 2
+    return tiles
+
+
+def doubled_up(array, axis, dim):
+    return in_order(grow_blocks(array, axis), dim)
 
 
 def shards(inputs, cand_user, event_user, event_count, w_qu, keys, values, gain, w_out):
@@ -22,7 +43,7 @@
     gate_values = jax.nn.silu(
         jnp.dot(inputs, gate_weight, preferred_element_type=jnp.float32)
     ).astype(jnp.bfloat16)
-    gathered_rows = lax.all_gather(inputs, "events", axis=0, tiled=True)
+    gathered_rows = doubled_up(inputs, "events", 0)
     queries = jax.nn.silu(
         jnp.dot(gathered_rows, query_weight, preferred_element_type=jnp.float32)
     ).astype(jnp.bfloat16)

time: 144 us -> 125 us (0.87)
  blocking collectives: 35.2 us -> 2.46 us
  starting transfers between devices: 0.04 us -> 7.31 us
  waiting for transfers between devices: 80.5 us -> 86.9 us
    all_gather x1 -> x0, blocking collectives: 32.8 us -> none  [shards(): gathered_rows = lax.all_gather(inputs, 'events', axis=0, tiled=True)]
    ppermute x0 -> x3, waiting for transfers between devices: none -> 7.49 us  [grow_blocks(): theirs = lax.ppermute(tiles, axis, [(i, i ^ apart) for i in range(size)])]
    ppermute x0 -> x3, starting transfers between devices: none -> 7.26 us  [grow_blocks(): theirs = lax.ppermute(tiles, axis, [(i, i ^ apart) for i in range(size)])]
  transfers between devices with their start and end apart: 2 -> 5, of which waited for: 2 -> 4; matrix products, arithmetic and copies ran while one was open for 0% -> 3% of each run, Pallas kernels for 0% -> 0%
where the time goes in v1:
time: 125 us
  waiting for transfers between devices  86.9 us (70%)
  between operations  14.1 us (11%)
  starting transfers between devices  7.31 us (6%)
  local copies, waits for them, and re-layouts  6 us (5%)
  matrix products  5.53 us (4%)
  other arithmetic  2.55 us (2%)
  blocking collectives  2.46 us (2%)
    reduce_scatter x1, waiting for transfers between devices, shards(): lax.psum_scatter(stacked.reshape(row_count * lax.axis_size('events'), loc...  62.4 us
    psum x1, waiting for transfers between devices, shards(): summed_heads = lax.psum(projected, 'heads')  16.9 us
    ppermute x3, waiting for transfers between devices, grow_blocks(): theirs = lax.ppermute(tiles, axis, [(i, i ^ apart) for i in range(size)])  7.49 us
    ppermute x3, starting transfers between devices, grow_blocks(): theirs = lax.ppermute(tiles, axis, [(i, i ^ apart) for i in range(size)])  7.26 us
    dot_general x1, matrix products, attend_rows(): jnp.einsum('hce,ehd->chd', attn_weights, value_heads, preferred_element_t...  2.64 us
  transfers between devices with their start and end apart: 5, of which 4 were waited for; matrix products, arithmetic and copies ran while one was open for 3% of the time, Pallas kernels for 0%

profile of v1, /device:TPU:0, one launch (start us, length us, event | category | flops | bytes accessed | tf_op | source)
XLA Modules:
  0.0 124.9 jit_solution(10235194845936673603)
XLA Ops:
  6.5 0.0 copy-start
  6.5 0.0 reduce-scatter.2.cloned.1.call-start
  6.5 3.0 %collective-permute-start = (bf16[1,16,1024]{2,1,0:T(8,128)(2,1)}, bf16[1,16,1024]{2,1,0:T(8,128)(2,1)S(1)}, u32[]{:S(2)}, u32[]{:S(2)}) collective-permute-start(bf16[1,16,1024]{2,1,0:T(8,128)(2,1)} %bitcast.35), channel_id=1, source_target_pairs={{0,2},{2,0},{4,6},{6,4},{8,10},{10,8},{12,14},{14,12},{1,3},{3,1},... | collective-permute-start | bytes 98312 | tf_op jit(solution)/shard_map/ppermute | solution.py:22
  10.2 2.0 %copy.14 = bf16[512,512]{0,1:T(8,128)(2,1)} copy(bf16[512,512]{1,0:T(8,128)(2,1)} %param.15) | data formatting | bytes 1048576 | tf_op jit(solution)/shard_map/reshape | solution.py:53
  12.2 0.0 copy-start.1
  12.2 0.0 copy-start.2
  12.2 0.0 copy-start.4
  12.2 2.2 %copy.17 = bf16[128,8,2,512]{3,1,2,0:T(8,128)(2,1)S(1)} copy(bf16[128,8,2,512]{3,2,1,0:T(2,128)(2,1)} %bitcast.33) | data formatting | bytes 4194304
  14.4 0.0 collective-permute-done
  14.4 0.0 copy-done.1
  14.4 1.6 %collective-permute-start.1 = (bf16[2,16,1024]{2,1,0:T(8,128)(2,1)S(1)}, bf16[2,16,1024]{2,1,0:T(8,128)(2,1)S(1)}, u32[]{:S(2)}, u32[]{:S(2)}) collective-permute-start(bf16[2,16,1024]{2,1,0:T(8,128)(2,1)S(1)} %pad_maximum_fusion.2), channel_id=1, source_target_pairs={{0,4},{2,6},{4,0},{6,2},{8,12},{10,14},{12,8},{14,10},{1,5},{3,7},... | collective-permute-start | bytes 196616 | tf_op jit(solution)/shard_map/ppermute | solution.py:22
  16.1 2.7 %collective-permute-done.1 = bf16[2,16,1024]{2,1,0:T(8,128)(2,1)S(1)} collective-permute-done((bf16[2,16,1024]{2,1,0:T(8,128)(2,1)S(1)}, bf16[2,16,1024]{2,1,0:T(8,128)(2,1)S(1)}, u32[]{:S(2)}, u32[]{:S(2)}) %collective-permute-start.1) | collective-permute-done | bytes 65568 | tf_op jit(solution)/shard_map/ppermute | solution.py:22
  18.8 2.7 %collective-permute-start.2 = (bf16[4,16,1024]{2,1,0:T(8,128)(2,1)S(1)}, bf16[4,16,1024]{2,1,0:T(8,128)(2,1)S(1)}, u32[]{:S(2)}, u32[]{:S(2)}) collective-permute-start(bf16[4,16,1024]{2,1,0:T(8,128)(2,1)S(1)} %pad_maximum_fusion.1), channel_id=1, source_target_pairs={{0,8},{2,10},{4,12},{6,14},{8,0},{10,2},{12,4},{14,6},{1,9},{3,11}... | collective-permute-start | bytes 393224 | tf_op jit(solution)/shard_map/ppermute | solution.py:22
  21.5 0.0 copy-done.2
  21.5 0.0 copy-done.4
  21.5 0.1 and_convert_fusion
  21.6 4.8 %collective-permute-done.2 = bf16[4,16,1024]{2,1,0:T(8,128)(2,1)S(1)} collective-permute-done((bf16[4,16,1024]{2,1,0:T(8,128)(2,1)S(1)}, bf16[4,16,1024]{2,1,0:T(8,128)(2,1)S(1)}, u32[]{:S(2)}, u32[]{:S(2)}) %collective-permute-start.2) | collective-permute-done | bytes 131104 | tf_op jit(solution)/shard_map/ppermute | solution.py:22
  26.4 1.0 fusion.14
  27.5 0.0 copy-start.3
  27.5 2.6 %fusion.4 = f32[4,128,128]{1,2,0:T(8,128)} fusion(bf16[512,4,128]{0,2,1:T(8,128)(2,1)} %bitcast.34, f32[128,512]{1,0:T(8,128)S(1)} %and_convert_fusion, bf16[16,4,8,128]{3,2,1,0:T(8,128)(2,1)} %fusion.14, bf16[512,512]{1,0:T(8,128)(2,1)} %param.14), kind=kOutput, calls=%fused_computation.6 | convolution fusion | flops 136052736 | bytes 1703936 | tf_op jit(solution)/shard_map/while/body/eval_jaxpr/hce,ehd->chd/dot_general | solution.py:66
  30.1 1.8 %copy.13 = f32[128,512]{1,0:T(8,128)} copy(f32[128,512]{0,1:T(8,128)} %bitcast.36) | data formatting | bytes 524288 | tf_op jit(solution)/shard_map/reshape | solution.py:82
  31.9 0.0 reduce-scatter.2.cloned.1.call-update
  31.9 0.0 all-reduce.3.cloned.1.call-start
  32.0 62.4 %reduce-scatter.2.cloned.1.call-done = f32[16,512]{1,0:T(8,128)} async-done(((f32[128,512]{1,0:T(8,128)}), f32[16,512]{1,0:T(8,128)}) %reduce-scatter.2.cloned.1.call-update) | async-done | bytes 32784 | tf_op jit(solution)/shard_map/reduce_scatter | solution.py:81
  94.4 0.9 fusion.38
  95.3 2.5 %all-reduce = (f32[16]{0:T(128)S(1)}, f32[16]{0:T(128)S(1)}) all-reduce(f32[16]{0:T(128)S(1)} %get-tuple-element.20, f32[16]{0:T(128)S(1)} %get-tuple-element.19), channel_id=1, replica_groups=mesh['groups'=2,'events'=8,'heads'=2] {'heads'}, use_global_device_ids=true, to_apply=%region_4.5 | all-reduce | flops 32 | bytes 256 | tf_op jit(solution)/shard_map/psum | solution.py:89
  97.7 0.0 copy-done
  97.7 0.0 copy-done.3
  97.8 1.9 %fusion.26 = f32[16,1024]{1,0:T(8,128)} fusion(bf16[512,1024]{1,0:T(8,128)(2,1)S(1)} %copy-done, bf16[16,1024]{1,0:T(8,128)(2,1)S(1)} %copy-done.1, bf16[1024,1024]{1,0:T(8,128)(2,1)S(1)} %bitcast.32, f32[16,512]{1,0:T(8,128)} %reduce-scatter.2.cloned.1.call-done, f32[512]{0:T(512)S(1)} %copy-done.3, f32[16]{0:T(128)S(1)} %get-tuple-element.40, ...), kind=kOutput, calls=%fused_computation.27 | convolution fusion | flops 33644544 | bytes 2231296 | tf_op jit(solution)/shard_map/dot_general | solution.py:94
  99.6 0.0 all-reduce.3.cloned.1.call-update
  99.6 16.9 %all-reduce.3.cloned.1.call-done = f32[16,1024]{1,0:T(8,128)} async-done(((f32[16,1024]{1,0:T(8,128)}), f32[16,1024]{1,0:T(8,128)}) %all-reduce.3.cloned.1.call-update) | async-done | bytes 65552 | tf_op jit(solution)/shard_map/psum | solution.py:95
  116.6 1.5 %add_convert_fusion = bf16[16,1024]{1,0:T(8,128)(2,1)} fusion(f32[16,1024]{1,0:T(8,128)} %all-reduce.3.cloned.1.call-done, bf16[16,1024]{1,0:T(8,128)(2,1)S(1)} %copy-done.1), kind=kLoop, calls=%fused_computation.22 | loop fusion | flops 49152 | bytes 131072 | tf_op jit(solution)/shard_map/convert_element_type | solution.py:96
  (8 shorter events, 0.1 us)
Async XLA Ops:
  6.5 91.2 %copy-start = (bf16[512,1024]{1,0:T(8,128)(2,1)S(1)}, bf16[512,1024]{1,0:T(8,128)(2,1)}, u32[]{:S(2)}) copy-start(bf16[512,1024]{1,0:T(8,128)(2,1)} %param.17) | copy-start | bytes 3145732
  6.5 87.9 %reduce-scatter.2.cloned.1.call-start = ((), (), s32[]{:S(2)}) async-start(), calls=%async_computation.1 | async-start | bytes 294912 | tf_op jit(solution)/shard_map/reduce_scatter | solution.py:81
  6.5 7.8 %collective-permute-start = (bf16[1,16,1024]{2,1,0:T(8,128)(2,1)}, bf16[1,16,1024]{2,1,0:T(8,128)(2,1)S(1)}, u32[]{:S(2)}, u32[]{:S(2)}) collective-permute-start(bf16[1,16,1024]{2,1,0:T(8,128)(2,1)} %bitcast.35), channel_id=1, source_target_pairs={{0,2},{2,0},{4,6},{6,4},{8,10},{10,8},{12,14},{14,12},{1,3},{3,1},... | collective-permute-start | bytes 98312 | tf_op jit(solution)/shard_map/ppermute | solution.py:22
  12.2 2.2 %copy-start.1 = (bf16[16,1024]{1,0:T(8,128)(2,1)S(1)}, bf16[16,1024]{1,0:T(8,128)(2,1)}, u32[]{:S(2)}) copy-start(bf16[16,1024]{1,0:T(8,128)(2,1)} %param.9) | copy-start | bytes 98308
  12.2 9.3 %copy-start.2 = (s32[512]{0:T(512)S(1)}, s32[512]{0:T(512)}, u32[]{:S(2)}) copy-start(s32[512]{0:T(512)} %param.11) | copy-start | bytes 6148
  12.2 9.3 %copy-start.4 = (s32[128]{0:T(128)S(1)}, s32[128]{0:T(128)}, u32[]{:S(2)}) copy-start(s32[128]{0:T(128)} %param.10) | copy-start | bytes 1540
  14.4 4.3 %collective-permute-start.1 = (bf16[2,16,1024]{2,1,0:T(8,128)(2,1)S(1)}, bf16[2,16,1024]{2,1,0:T(8,128)(2,1)S(1)}, u32[]{:S(2)}, u32[]{:S(2)}) collective-permute-start(bf16[2,16,1024]{2,1,0:T(8,128)(2,1)S(1)} %pad_maximum_fusion.2), channel_id=1, source_target_pairs={{0,4},{2,6},{4,0},{6,2},{8,12},{10,14},{12,8},{14,10},{1,5},{3,7},... | collective-permute-start | bytes 196616 | tf_op jit(solution)/shard_map/ppermute | solution.py:22
  18.8 7.6 %collective-permute-start.2 = (bf16[4,16,1024]{2,1,0:T(8,128)(2,1)S(1)}, bf16[4,16,1024]{2,1,0:T(8,128)(2,1)S(1)}, u32[]{:S(2)}, u32[]{:S(2)}) collective-permute-start(bf16[4,16,1024]{2,1,0:T(8,128)(2,1)S(1)} %pad_maximum_fusion.1), channel_id=1, source_target_pairs={{0,8},{2,10},{4,12},{6,14},{8,0},{10,2},{12,4},{14,6},{1,9},{3,11}... | collective-permute-start | bytes 393224 | tf_op jit(solution)/shard_map/ppermute | solution.py:22
  27.5 70.3 %copy-start.3 = (f32[512]{0:T(512)S(1)}, f32[512]{0:T(512)}, u32[]{:S(2)}) copy-start(f32[512]{0:T(512)} %param.16) | copy-start | bytes 6148
  31.9 84.6 %all-reduce.3.cloned.1.call-start = ((), (), s32[]{:S(2)}) async-start(), calls=%async_computation.2 | async-start | bytes 131072 | tf_op jit(solution)/shard_map/psum | solution.py:95
Sparse Core Ops, SparseCore 0:
  32.0 62.3 reduce-scatter.1
  99.8 16.7 all-reduce.2
